TPU v7x, 128 devices: a whole 4x4x4 slice. The times are simulated.
128 devices in a mesh: seq: 32 (over y, z, core), head: 4 (over x).
Axes of the slice: x: 4, y: 4, z: 4, core: 2. Of those that a mesh axis runs over, the one named last changes fastest.
Arguments:
- queries: bfloat16 [8192, 2048], P('seq', 'head'), parts along dimension 1, may hold values from -6 to 6
- keys: bfloat16 [8192, 512], P('seq', 'head'), parts along dimension 1, may hold values from -6 to 6
- values: bfloat16 [8192, 512], P('seq', 'head'), parts along dimension 1, may hold values from -6 to 6
- grad_out: bfloat16 [8192, 2048], P('seq', 'head'), parts along dimension 1, may hold values from -6 to 6
- lengths: int32 [16], replicated, may hold values from 1 to 2048, 8192 in all
- send_order: int32 [32, 256], replicated, may hold values from 0 to 255, each once within a row
Outputs:
- attended: float32 [8192, 2048], P('seq', 'head'), parts along dimension 1
- grad_queries: float32 [8192, 2048], P('seq', 'head'), parts along dimension 1
- grad_keys: float32 [8192, 512], P('seq', 'head'), parts along dimension 1
- grad_values: float32 [8192, 512], P('seq', 'head'), parts along dimension 1
There are 4 independent parts, one for each index of `head`. A program takes and returns all parts, laid end to end along the dimension named above; an argument that names none is the same for every part. Nothing has to cross between parts.
Inputs may be any that keep to these rules, and one draw needn't show every extreme that they name: `lengths`: they sum to 8192; the longest is exactly 2048. `send_order`: each row is a permutation of 0 to 255.
All inputs are finite; a program needn't handle non-finite values.
Results may differ from a plain program's by a relative error of at most 0.039.
Values may be sent and summed in bfloat16 or wider, within the bound.
No kernel may reach another device: no remote copies, remote signals or barrier semaphores. Data moves between devices by JAX's collectives and lax.ppermute only.
A program may use at most 64 MiB of HBM per device.

v0:
```python
import math

import jax
import jax.numpy as jnp
from jax import lax
from jax.sharding import PartitionSpec as P

masked_value = -1e30


def doc_index(positions, bounds):
    return jnp.sum((positions[:, None] >= bounds[None, :]).astype(jnp.int32), axis=1)


def visible(query_pos, query_doc, key_pos, bounds):
    key_doc = doc_index(key_pos, bounds)
    return ((query_doc[:, None] == key_doc[None, :]) & (key_pos[None, :] <= query_pos[:, None]))[
        :, None, :
    ]


def block_scores(query_heads, key_block, allowed, score_scale):
    products = (
        jnp.einsum("bhd,td->bht", query_heads, key_block, preferred_element_type=jnp.float32)
        * score_scale
    )
    return jnp.where(allowed, products, masked_value)


def key_blocks(key_piece, value_piece):
    piece_rows = key_piece.shape[0]
    block_rows = math.gcd(piece_rows, 512)
    block_count = piece_rows // block_rows
    offsets = block_rows * jnp.arange(block_count, dtype=jnp.int32)
    stacked = (
        key_piece.reshape(block_count, block_rows, key_piece.shape[1]),
        value_piece.reshape(block_count, block_rows, value_piece.shape[1]),
        offsets,
    )
    return (stacked, block_rows)


def forward_piece(run_state, key_piece, value_piece, context):
    query_heads, query_pos, query_doc, bounds, score_scale = context
    stacked, block_rows = key_blocks(key_piece, value_piece)

    def forward_update(loop_state, block_item):
        run_max, run_total, weighted = loop_state
        key_block, value_block, offset = block_item
        allowed = visible(
            query_pos, query_doc, offset + jnp.arange(block_rows, dtype=jnp.int32), bounds
        )
        scores = block_scores(query_heads, key_block, allowed, score_scale)
        new_max = jnp.maximum(run_max, jnp.max(scores, axis=2))
        exp_weights = jnp.where(allowed, jnp.exp(scores - new_max[:, :, None]), 0.0)
        rescale = jnp.exp(run_max - new_max)
        run_total = run_total * rescale + jnp.sum(exp_weights, axis=2)
        weighted = weighted * rescale[:, :, None] + jnp.einsum(
            "bht,td->bhd",
            exp_weights.astype(jnp.bfloat16),
            value_block,
            preferred_element_type=jnp.float32,
        )
        return ((new_max, run_total, weighted), None)

    run_state, _ = lax.scan(forward_update, run_state, stacked)
    return run_state


def backward_piece(key_piece, value_piece, context):
    query_heads, grad_heads, query_pos, query_doc, bounds, score_scale, log_total, out_dot = context
    stacked, block_rows = key_blocks(key_piece, value_piece)

    def backward_update(query_sum, block_item):
        key_block, value_block, offset = block_item
        allowed = visible(
            query_pos, query_doc, offset + jnp.arange(block_rows, dtype=jnp.int32), bounds
        )
        scores = block_scores(query_heads, key_block, allowed, score_scale)
        weights = jnp.where(allowed, jnp.exp(scores - log_total[:, :, None]), 0.0)
        grad_dots = jnp.einsum(
            "bhd,td->bht", grad_heads, value_block, preferred_element_type=jnp.float32
        )
        score_grads = (weights * (grad_dots - out_dot[:, :, None])).astype(jnp.bfloat16)
        query_sum = query_sum + jnp.einsum(
            "bht,td->bhd", score_grads, key_block, preferred_element_type=jnp.float32
        )
        key_term = (
            jnp.einsum("bht,bhd->td", score_grads, query_heads, preferred_element_type=jnp.float32)
            * score_scale
        )
        value_term = jnp.einsum(
            "bht,bhd->td",
            weights.astype(jnp.bfloat16),
            grad_heads,
            preferred_element_type=jnp.float32,
        )
        return (query_sum, (key_term, value_term))

    zero_query = jnp.zeros(query_heads.shape, jnp.float32)
    query_add, (key_terms, value_terms) = lax.scan(backward_update, zero_query, stacked)
    piece_rows = key_piece.shape[0]
    return (query_add, key_terms.reshape(piece_rows, -1), value_terms.reshape(piece_rows, -1))


def per_device(queries, keys, values, grad_out, lengths, send_order):
    shard_count = lax.axis_size("seq")
    my_index = lax.axis_index("seq")
    tok_rows, head_dim = keys.shape
    group_rows = tok_rows // shard_count
    head_count = queries.shape[1] // head_dim
    score_scale = 1.0 / math.sqrt(head_dim)
    bounds = jnp.cumsum(lengths)
    own_order = lax.dynamic_index_in_dim(send_order, my_index, 0, keepdims=False)
    outgoing = jnp.take(queries, own_order, axis=0)
    picked = lax.all_to_all(outgoing, "seq", split_axis=0, concat_axis=0, tiled=True)
    columns = lax.dynamic_slice_in_dim(send_order, my_index * group_rows, group_rows, 1)
    query_pos = (jnp.arange(shard_count, dtype=jnp.int32)[:, None] * tok_rows + columns).reshape(
        tok_rows
    )
    query_doc = doc_index(query_pos, bounds)
    query_heads = picked.reshape(tok_rows, head_count, head_dim)
    grad_heads = grad_out.reshape(tok_rows, head_count, head_dim)
    context = (query_heads, query_pos, query_doc, bounds, score_scale)
    start_state = (
        jnp.full((tok_rows, head_count), masked_value, jnp.float32),
        jnp.zeros((tok_rows, head_count), jnp.float32),
        jnp.zeros((tok_rows, head_count, head_dim), jnp.float32),
    )
    piece_pair = (
        lax.all_gather(keys, "seq", axis=0, tiled=True),
        lax.all_gather(values, "seq", axis=0, tiled=True),
    )
    run_max, run_total, weighted = forward_piece(start_state, piece_pair[0], piece_pair[1], context)
    attended = weighted / run_total[:, :, None]
    attended_low = attended.astype(jnp.bfloat16)
    log_total = run_max + jnp.log(run_total)
    out_dot = jnp.sum(grad_heads.astype(jnp.float32) * attended_low.astype(jnp.float32), axis=2)
    grad_context = (
        query_heads,
        grad_heads,
        query_pos,
        query_doc,
        bounds,
        score_scale,
        log_total,
        out_dot,
    )
    piece_pair = (
        lax.all_gather(keys, "seq", axis=0, tiled=True),
        lax.all_gather(values, "seq", axis=0, tiled=True),
    )
    query_add, key_part, value_part = backward_piece(piece_pair[0], piece_pair[1], grad_context)
    key_all = key_part
    value_all = value_part
    query_sum, key_all, value_all = (query_add, key_all, value_all)
    key_grad, value_grad = (
        lax.psum_scatter(key_all, "seq", scatter_dimension=0, tiled=True),
        lax.psum_scatter(value_all, "seq", scatter_dimension=0, tiled=True),
    )
    grad_queries = (query_sum * score_scale).reshape(tok_rows, head_count * head_dim)
    return (attended.reshape(tok_rows, head_count * head_dim), grad_queries, key_grad, value_grad)


def solution(mesh):
    placed = (P("seq", "head"), P("seq", "head"), P("seq", "head"), P("seq", "head"), P(), P())
    return jax.shard_map(
        per_device,
        mesh=mesh,
        in_specs=placed,
        out_specs=(P("seq", "head"), P("seq", "head"), P("seq", "head"), P("seq", "head")),
        check_vma=False,
    )
```

profile of v0, /device:TPU:119, one launch (start us, length us, event | category | flops | bytes accessed | tf_op | source)
XLA Modules:
  0.0 490.4 jit_solution(17738057707198617605)
XLA Ops:
  12.2 7.4 %all-to-all-start = ((bf16[32,8,512]{2,1,0:T(8,128)(2,1)}), bf16[32,8,512]{2,1,0:T(8,128)(2,1)S(1)}, u32[]{:S(2)}, u32[]{:S(2)}) async-start(bf16[32,8,512]{2,1,0:T(8,128)(2,1)} %bitcast_select_fusion.2), calls=%async_computation | async-start | bytes 524288 | tf_op jit(solution)/shard_map/all_to_all | solution.py:116
  20.7 4.1 all-to-all-done
  25.0 28.6 %all-gather.3.cloned.1.call-done = bf16[8192,128]{1,0:T(8,128)(2,1)} async-done(((bf16[256,128]{1,0:T(8,128)(2,1)}), bf16[8192,128]{1,0:T(8,128)(2,1)}) %all-gather.3.cloned.1.call-update) | async-done | bytes 2097168 | tf_op jit(solution)/shard_map/all_gather | solution.py:131
  53.6 45.3 %all-gather.5.cloned.1.call-done = bf16[8192,128]{1,0:T(8,128)(2,1)} async-done(((bf16[256,128]{1,0:T(8,128)(2,1)}), bf16[8192,128]{1,0:T(8,128)(2,1)}) %all-gather.5.cloned.1.call-update) | async-done | bytes 2097168 | tf_op jit(solution)/shard_map/all_gather | solution.py:132
  98.9 85.3 %while.32 = (s32[]{:T(128)}, f32[256,4]{0,1:T(4,128)S(1)}, f32[256,4]{0,1:T(4,128)S(1)}, f32[256,4,128]{2,0,1:T(8,128)S(1)}, s32[256]{0:T(256)S(1)}, /*index=5*/...) while((s32[]{:T(128)}, f32[256,4]{0,1:T(4,128)S(1)}, ...), condition=%wide.wide.region_6.7_spmd.clone, body=%wide.wide.region_2.6_spmd.clone.sunk | while | flops 276067328 | bytes 8466673 | solution.py:66
  102.4 1.8 convolution_add_fusion.6
  107.7 1.8 convolution_add_fusion.6
  113.0 1.8 convolution_add_fusion.6
  118.3 1.8 convolution_add_fusion.6
  123.7 1.8 convolution_add_fusion.6
  129.0 1.8 convolution_add_fusion.6
  134.3 1.8 convolution_add_fusion.6
  139.7 1.8 convolution_add_fusion.6
  145.0 1.8 convolution_add_fusion.6
  150.3 1.8 convolution_add_fusion.6
  155.7 1.8 convolution_add_fusion.6
  161.0 1.8 convolution_add_fusion.6
  166.3 1.8 convolution_add_fusion.6
  171.7 1.8 convolution_add_fusion.6
  177.0 1.8 convolution_add_fusion.6
  182.3 1.8 convolution_add_fusion.6
  184.4 133.8 %while.33 = (s32[]{:T(128)}, f32[256,4,128]{2,0,1:T(8,128)S(1)}, f32[16,512,128]{2,1,0:T(8,128)}, f32[16,512,128]{2,1,0:T(8,128)}, s32[256]{0:T(256)S(1)}, /*ind...) while((s32[]{:T(128)}, f32[256,4,128]{2,0,1:T(8,128)S(1)}, ...), condition=%wide.wide.region_10.11_spmd.clone, body=%wide.wide.region_8.10_spmd.clone.sunk | while | flops 676028416 | bytes 12734739 | solution.py:101
  186.0 1.6 fusion.101
  189.0 1.6 convolution_add_fusion.7
  194.3 1.6 fusion.101
  197.3 1.6 convolution_add_fusion.7
  202.7 1.6 fusion.101
  211.0 1.6 fusion.101
  219.4 1.6 fusion.101
  227.8 1.6 fusion.101
  236.2 1.6 fusion.101
  244.5 1.6 fusion.101
  247.5 1.6 convolution_add_fusion.7
  252.9 1.6 fusion.101
  255.9 1.6 convolution_add_fusion.7
  261.3 1.6 fusion.101
  269.6 1.6 fusion.101
  272.6 1.6 convolution_add_fusion.7
  278.0 1.6 fusion.101
  286.4 1.6 fusion.101
  289.3 1.6 convolution_add_fusion.7
  294.7 1.6 fusion.101
  297.7 1.6 convolution_add_fusion.7
  303.1 1.6 fusion.101
  306.0 1.6 convolution_add_fusion.7
  311.4 1.6 fusion.101
  320.7 77.3 %reduce-scatter.5.cloned.1.call-done = f32[256,128]{1,0:T(8,128)} async-done(((f32[8192,128]{1,0:T(8,128)}), f32[256,128]{1,0:T(8,128)}) %reduce-scatter.5.cloned.1.call-update) | async-done | bytes 131088 | tf_op jit(solution)/shard_map/reduce_scatter | solution.py:159
  398.0 85.8 %reduce-scatter.3.cloned.1.call-done = f32[256,128]{1,0:T(8,128)} async-done(((f32[8192,128]{1,0:T(8,128)}), f32[256,128]{1,0:T(8,128)}) %reduce-scatter.3.cloned.1.call-update) | async-done | bytes 131088 | tf_op jit(solution)/shard_map/reduce_scatter | solution.py:158
  (314 shorter events, 159.5 us)
Async XLA Ops:
  7.2 3.1 copy-start
  7.2 12.5 %copy-start.3 = (s32[32,256]{1,0:T(8,128)S(1)}, s32[32,256]{1,0:T(8,128)}, u32[]{:S(2)}) copy-start(s32[32,256]{1,0:T(8,128)} %param.15) | copy-start | bytes 98308
  7.2 12.9 %copy-start.4 = (s32[16]{0:T(128)S(1)}, s32[16]{0:T(128)}, u32[]{:S(2)}) copy-start(s32[16]{0:T(128)} %param.14) | copy-start | bytes 196
  7.2 13.1 %copy-start.1 = (bf16[256,512]{1,0:T(8,128)(2,1)S(1)}, bf16[256,512]{1,0:T(8,128)(2,1)}, u32[]{:S(2)}) copy-start(bf16[256,512]{1,0:T(8,128)(2,1)} %param.13) | copy-start | bytes 786436
  7.2 46.3 %all-gather.3.cloned.1.call-start = ((), (), s32[]{:S(2)}) async-start(), calls=%async_computation.3 | async-start | bytes 2162688 | tf_op jit(solution)/shard_map/all_gather | solution.py:131
  7.9 90.9 %all-gather.5.cloned.1.call-start = ((), (), s32[]{:S(2)}) async-start(), calls=%async_computation.4 | async-start | bytes 2162688 | tf_op jit(solution)/shard_map/all_gather | solution.py:132
  12.2 12.7 %all-to-all-start = ((bf16[32,8,512]{2,1,0:T(8,128)(2,1)}), bf16[32,8,512]{2,1,0:T(8,128)(2,1)S(1)}, u32[]{:S(2)}, u32[]{:S(2)}) async-start(bf16[32,8,512]{2,1,0:T(8,128)(2,1)} %bitcast_select_fusion.2), calls=%async_computation | async-start | bytes 524288 | tf_op jit(solution)/shard_map/all_to_all | solution.py:116
  19.6 378.4 %reduce-scatter.5.cloned.1.call-start = ((), (), s32[]{:S(2)}) async-start(), calls=%async_computation.6 | async-start | bytes 4325376 | tf_op jit(solution)/shard_map/reduce_scatter | solution.py:159
  19.8 79.1 %copy-start.2 = (s32[32,8]{1,0:T(8,128)}, s32[32,8]{1,0:T(8,128)S(1)}, u32[]{:S(2)}) copy-start(s32[32,8]{1,0:T(8,128)S(1)} %dynamic-slice_add_fusion) | copy-start | bytes 3076
  318.3 165.6 %reduce-scatter.3.cloned.1.call-start = ((), (), s32[]{:S(2)}) async-start(), calls=%async_computation.5 | async-start | bytes 4325376 | tf_op jit(solution)/shard_map/reduce_scatter | solution.py:158
Sparse Core Ops, SparseCore 0:
  10.3 43.2 all-gather.2
  55.8 42.9 all-gather.4
  318.4 79.5 reduce-scatter.4
  402.1 81.6 reduce-scatter.2
where the time goes:
time: 498 us; the launch traced here: 490 us
  waiting for transfers between devices  243 us (49%)
  matrix products  160 us (32%)
  other arithmetic  41.9 us (8%)
  local copies, waits for them, and re-layouts  22.7 us (5%)
  between operations  14 us (3%)
  starting transfers between devices  7.55 us (2%)
    reduce_scatter x1, waiting for transfers between devices, per_device(): lax.psum_scatter(key_all, 'seq', scatter_dimension=0, tiled=True)  85.8 us
    reduce_scatter x1, waiting for transfers between devices, per_device(): lax.psum_scatter(value_all, 'seq', scatter_dimension=0, tiled=True)  77.3 us
    dot_general x32, matrix products, block_scores(): jnp.einsum('bhd,td->bht', query_heads, key_block, preferred_element_type=...  47.9 us
    all_gather x1, waiting for transfers between devices, per_device(): lax.all_gather(values, 'seq', axis=0, tiled=True)  45.3 us
    dot_general x16, matrix products, forward_update(): jnp.einsum('bht,td->bhd', exp_weights.astype(jnp.bfloat16), value_block,...  28.7 us
    all_gather x1, waiting for transfers between devices, per_device(): lax.all_gather(keys, 'seq', axis=0, tiled=True)  28.6 us
    dot_general x16, matrix products, backward_update(): jnp.einsum('bht,td->bhd', score_grads, key_block, preferred_element_type=...  24.8 us
    dot_general x16, matrix products, backward_update(): jnp.einsum('bhd,td->bht', grad_heads, value_block, preferred_element_type...  21.5 us
  transfers between devices with their start and end apart: 5, of which 5 were waited for; matrix products, arithmetic and copies ran while one was open for 1% of the time, Pallas kernels for 0%

commit v1 on v0

v1 whole, which is shorter than its diff:
```python
import math

import jax
import jax.numpy as jnp
from jax import lax
from jax.sharding import PartitionSpec as P

masked_value = -1e30
LONGEST = 2048


def doc_index(positions, bounds):
    return jnp.sum((positions[:, None] >= bounds[None, :]).astype(jnp.int32), axis=1)


def per_device(queries, keys, values, grad_out, lengths, send_order):
    shard_count = lax.axis_size("seq")
    my_index = lax.axis_index("seq")
    tok_rows, head_dim = keys.shape
    head_count = queries.shape[1] // head_dim
    score_scale = 1.0 / math.sqrt(head_dim)
    halo = min(shard_count - 1, (LONGEST - 1 + tok_rows - 1) // tok_rows)
    bounds = jnp.cumsum(lengths)

    own_order = lax.dynamic_index_in_dim(send_order, my_index, 0, keepdims=False)
    query_rows = jnp.take(queries, own_order, axis=0)
    query_heads = query_rows.reshape(tok_rows, head_count, head_dim)
    query_pos = my_index * tok_rows + own_order
    query_doc = doc_index(query_pos, bounds)
    grad_rows = lax.all_to_all(grad_out, "seq", 0, 0, tiled=True)
    grad_heads = grad_rows.reshape(tok_rows, head_count, head_dim)

    pair = jnp.concatenate([keys, values], axis=1)
    blocks = [pair]
    for shift in range(1, halo + 1):
        blocks.append(
            lax.ppermute(pair, "seq", [(i, i + shift) for i in range(shard_count - shift)])
        )
    halo_pair = jnp.concatenate(blocks, axis=0)
    key_all = halo_pair[:, :head_dim]
    value_all = halo_pair[:, head_dim:]
    block_ids = jnp.repeat(jnp.arange(halo + 1, dtype=jnp.int32), tok_rows)
    key_pos = (my_index - block_ids) * tok_rows + jnp.tile(
        jnp.arange(tok_rows, dtype=jnp.int32), halo + 1
    )
    key_doc = doc_index(key_pos, bounds)
    allowed = (
        (query_doc[:, None] == key_doc[None, :])
        & (key_pos[None, :] <= query_pos[:, None])
        & (key_pos[None, :] >= 0)
    )[:, None, :]

    products = (
        jnp.einsum("bhd,td->bht", query_heads, key_all, preferred_element_type=jnp.float32)
        * score_scale
    )
    scores = jnp.where(allowed, products, masked_value)
    row_max = jnp.max(scores, axis=2)
    log_total = row_max + jnp.log(jnp.sum(jnp.exp(scores - row_max[:, :, None]), axis=2))
    weights = jnp.where(allowed, jnp.exp(scores - log_total[:, :, None]), 0.0)
    weights_low = weights.astype(jnp.bfloat16)
    attended = jnp.einsum(
        "bht,td->bhd", weights_low, value_all, preferred_element_type=jnp.float32
    )
    attended_low = attended.astype(jnp.bfloat16)
    out_dot = jnp.sum(grad_heads.astype(jnp.float32) * attended_low.astype(jnp.float32), axis=2)
    grad_dots = jnp.einsum(
        "bhd,td->bht", grad_heads, value_all, preferred_element_type=jnp.float32
    )
    score_grads = (weights * (grad_dots - out_dot[:, :, None])).astype(jnp.bfloat16)
    grad_query = (
        jnp.einsum("bht,td->bhd", score_grads, key_all, preferred_element_type=jnp.float32)
        * score_scale
    )
    key_term = (
        jnp.einsum("bht,bhd->td", score_grads, query_heads, preferred_element_type=jnp.float32)
        * score_scale
    )
    value_term = jnp.einsum(
        "bht,bhd->td", weights_low, grad_heads, preferred_element_type=jnp.float32
    )
    terms = jnp.concatenate([key_term, value_term], axis=1).reshape(halo + 1, tok_rows, -1)
    total = terms[0]
    for shift in range(1, halo + 1):
        total = total + lax.ppermute(
            terms[shift], "seq", [(i, i - shift) for i in range(shift, shard_count)]
        )
    key_grad = total[:, :head_dim]
    value_grad = total[:, head_dim:]

    row_outs = jnp.concatenate(
        [
            attended.reshape(tok_rows, head_count * head_dim),
            grad_query.reshape(tok_rows, head_count * head_dim),
        ],
        axis=1,
    )
    balanced = lax.all_to_all(row_outs, "seq", 0, 0, tiled=True)
    width = head_count * head_dim
    return (balanced[:, :width], balanced[:, width:], key_grad, value_grad)


def solution(mesh):
    placed = (P("seq", "head"), P("seq", "head"), P("seq", "head"), P("seq", "head"), P(), P())
    return jax.shard_map(
        per_device,
        mesh=mesh,
        in_specs=placed,
        out_specs=(P("seq", "head"), P("seq", "head"), P("seq", "head"), P("seq", "head")),
        check_vma=False,
    )
```

time: 498 us -> 137 us (0.28); the launches traced: 490 us -> 137 us
  waiting for transfers between devices: 243 us -> 29.4 us
  matrix products: 160 us -> 16.8 us
  starting transfers between devices: 7.55 us -> 62.1 us
  other arithmetic: 41.9 us -> 6.57 us
  between operations: 14 us -> 1 us
    reduce_scatter x2 -> x0, waiting for transfers between devices: 163 us -> none  [the longest x1 85.8 us: per_device(): lax.psum_scatter(key_all, 'seq', scatter_dimension=0, tiled=True)]
    dot_general x112 -> x6, matrix products: 160 us -> 16.8 us  [the longest x1 6.52 us: per_device(): jnp.einsum('bht,td->bhd', weights_low, value_all, preferred_element_type=...]
    all_gather x2 -> x0, waiting for transfers between devices: 73.9 us -> none  [the longest x1 45.3 us: per_device(): lax.all_gather(values, 'seq', axis=0, tiled=True)]
    ppermute x0 -> x16, starting transfers between devices: none -> 44.9 us  [the longest x8 23.7 us: per_device(): lax.ppermute(terms[shift], 'seq', [(i, i - shift) for i in range(shift, s...]
    ppermute x0 -> x16, waiting for transfers between devices: none -> 29.4 us  [the longest x8 27 us: per_device(): lax.ppermute(terms[shift], 'seq', [(i, i - shift) for i in range(shift, s...]
    add x50 -> x4, other arithmetic: 21.1 us -> 1.12 us  [the longest x1 1.1 us: per_device(): total + lax.ppermute(terms[shift], 'seq', [(i, i - shift) for i in range(...]
    dynamic_slice x33 -> x0, local copies, waits for them, and re-layouts: 19.4 us -> none  [the longest x32 18.7 us: forward_piece(): run_state, _ = lax.scan(forward_update, run_state, stacked)]
    all_to_all x1 -> x2, starting transfers between devices: 7.39 us -> 17.2 us  [the longest x1 8.63 us: per_device(): balanced = lax.all_to_all(row_outs, 'seq', 0, 0, tiled=True)]
  transfers between devices with their start and end apart: 5 -> 18, of which waited for: 5 -> 7; matrix products, arithmetic and copies ran while one was open for 1% -> 13% of each run, Pallas kernels for 0% -> 0%
where the time goes in v1:
time: 137 us
  starting transfers between devices  62.1 us (45%)
  waiting for transfers between devices  29.4 us (21%)
  local copies, waits for them, and re-layouts  20.6 us (15%)
  matrix products  16.8 us (12%)
  other arithmetic  6.57 us (5%)
    ppermute x8, waiting for transfers between devices, per_device(): lax.ppermute(terms[shift], 'seq', [(i, i - shift) for i in range(shift, s...  27 us
    ppermute x8, starting transfers between devices, per_device(): lax.ppermute(terms[shift], 'seq', [(i, i - shift) for i in range(shift, s...  23.7 us
    ppermute x8, starting transfers between devices, per_device(): lax.ppermute(pair, 'seq', [(i, i + shift) for i in range(shard_count - sh...  21.2 us
    unnamed x22, local copies, waits for them, and re-layouts  10.4 us
    all_to_all x1, starting transfers between devices, per_device(): balanced = lax.all_to_all(row_outs, 'seq', 0, 0, tiled=True)  8.63 us
    all_to_all x1, starting transfers between devices, per_device(): grad_rows = lax.all_to_all(grad_out, 'seq', 0, 0, tiled=True)  8.57 us
    dot_general x1, matrix products, per_device(): jnp.einsum('bht,td->bhd', weights_low, value_all, preferred_element_type=...  6.52 us
    dot_general x1, matrix products, per_device(): jnp.einsum('bhd,td->bht', query_heads, key_all, preferred_element_type=jn...  3.2 us
  transfers between devices with their start and end apart: 18, of which 7 were waited for; matrix products, arithmetic and copies ran while one was open for 13% of the time, Pallas kernels for 0%

profile of v1, /device:TPU:119, one launch (start us, length us, event | category | flops | bytes accessed | tf_op | source)
XLA Modules:
  0.0 136.5 jit_solution(11314740068120277838)
XLA Ops:
  0.6 1.5 %constant_dynamic-update-slice_fusion.1 = (bf16[256,256]{1,0:T(8,128)(2,1)S(1)}, bf16[2304,256]{1,0:T(8,128)(2,1)}) fusion(bf16[256,128]{1,0:T(8,128)(2,1)} %param.7), kind=kLoop, calls=%fused_computation.55 | loop fusion | bytes 196608
  2.2 1.5 %constant_dynamic-update-slice_fusion = (bf16[256,256]{1,0:T(8,128)(2,1)S(1)}, bf16[2304,256]{1,0:T(8,128)(2,1)}) fusion(bf16[256,256]{1,0:T(8,128)(2,1)S(1)} %get-tuple-element.32, bf16[256,128]{1,0:T(8,128)(2,1)} %param.8, bf16[2304,256]{1,0:T(8,128)(2,1)} %get-tuple-element.33), kind=kLoop, calls=%fused_computation.54 | loop fusion | bytes 196608 | tf_op jit(solution)/shard_map/concatenate | solution.py:33
  3.7 2.1 %collective-permute-start = (bf16[256,256]{1,0:T(8,128)(2,1)S(1)}, bf16[256,256]{1,0:T(8,128)(2,1)S(1)}, u32[]{:S(2)}, u32[]{:S(2)}) collective-permute-start(bf16[256,256]{1,0:T(8,128)(2,1)S(1)} %get-tuple-element.30), channel_id=1, source_target_pairs={{0,4},{4,8},{8,12},{12,16},{16,20},{20,24},{24,28},{28,32},{32,36}... | collective-permute-start | bytes 393224 | tf_op jit(solution)/shard_map/ppermute | solution.py:37
  5.8 3.5 %collective-permute-start.1 = (bf16[256,256]{1,0:T(8,128)(2,1)S(1)}, bf16[256,256]{1,0:T(8,128)(2,1)S(1)}, u32[]{:S(2)}, u32[]{:S(2)}) collective-permute-start(bf16[256,256]{1,0:T(8,128)(2,1)S(1)} %get-tuple-element.30), channel_id=1, source_target_pairs={{0,8},{4,12},{8,16},{12,20},{16,24},{20,28},{24,32},{28,36},{32,40... | collective-permute-start | bytes 393224 | tf_op jit(solution)/shard_map/ppermute | solution.py:37
  9.3 3.6 %collective-permute-start.2 = (bf16[256,256]{1,0:T(8,128)(2,1)S(1)}, bf16[256,256]{1,0:T(8,128)(2,1)S(1)}, u32[]{:S(2)}, u32[]{:S(2)}) collective-permute-start(bf16[256,256]{1,0:T(8,128)(2,1)S(1)} %get-tuple-element.30), channel_id=1, source_target_pairs={{0,12},{4,16},{8,20},{12,24},{16,28},{20,32},{24,36},{28,40},{32,4... | collective-permute-start | bytes 393224 | tf_op jit(solution)/shard_map/ppermute | solution.py:37
  12.9 3.0 %collective-permute-start.3 = (bf16[256,256]{1,0:T(8,128)(2,1)S(1)}, bf16[256,256]{1,0:T(8,128)(2,1)S(1)}, u32[]{:S(2)}, u32[]{:S(2)}) collective-permute-start(bf16[256,256]{1,0:T(8,128)(2,1)S(1)} %get-tuple-element.30), channel_id=1, source_target_pairs={{0,16},{4,20},{8,24},{12,28},{16,32},{20,36},{24,40},{28,44},{32,4... | collective-permute-start | bytes 393224 | tf_op jit(solution)/shard_map/ppermute | solution.py:37
  15.9 1.9 %collective-permute-start.4 = (bf16[256,256]{1,0:T(8,128)(2,1)S(1)}, bf16[256,256]{1,0:T(8,128)(2,1)S(1)}, u32[]{:S(2)}, u32[]{:S(2)}) collective-permute-start(bf16[256,256]{1,0:T(8,128)(2,1)S(1)} %get-tuple-element.30), channel_id=1, source_target_pairs={{0,20},{4,24},{8,28},{12,32},{16,36},{20,40},{24,44},{28,48},{32,5... | collective-permute-start | bytes 393224 | tf_op jit(solution)/shard_map/ppermute | solution.py:37
  17.8 8.6 %all-to-all-start = ((bf16[32,8,512]{2,1,0:T(8,128)(2,1)}), bf16[32,8,512]{2,1,0:T(8,128)(2,1)S(1)}, u32[]{:S(2)}, u32[]{:S(2)}) async-start(bf16[32,8,512]{2,1,0:T(8,128)(2,1)} %bitcast.37), calls=%async_computation | async-start | bytes 524288 | tf_op jit(solution)/shard_map/all_to_all | solution.py:30
  26.4 0.7 copy.32
  27.4 0.7 compare_select_fusion
  28.9 1.2 gather_fusion
  30.2 3.1 %collective-permute-start.5 = (bf16[256,256]{1,0:T(8,128)(2,1)S(1)}, bf16[256,256]{1,0:T(8,128)(2,1)S(1)}, u32[]{:S(2)}, u32[]{:S(2)}) collective-permute-start(bf16[256,256]{1,0:T(8,128)(2,1)S(1)} %get-tuple-element.30), channel_id=1, source_target_pairs={{0,24},{4,28},{8,32},{12,36},{16,40},{20,44},{24,48},{28,52},{32,5... | collective-permute-start | bytes 393224 | tf_op jit(solution)/shard_map/ppermute | solution.py:37
  34.0 1.9 %collective-permute-start.6 = (bf16[256,256]{1,0:T(8,128)(2,1)S(1)}, bf16[256,256]{1,0:T(8,128)(2,1)S(1)}, u32[]{:S(2)}, u32[]{:S(2)}) collective-permute-start(bf16[256,256]{1,0:T(8,128)(2,1)S(1)} %get-tuple-element.30), channel_id=1, source_target_pairs={{0,28},{4,32},{8,36},{12,40},{16,44},{20,48},{24,52},{28,56},{32,6... | collective-permute-start | bytes 393224 | tf_op jit(solution)/shard_map/ppermute | solution.py:37
  36.6 2.1 %collective-permute-start.7 = (bf16[256,256]{1,0:T(8,128)(2,1)S(1)}, bf16[256,256]{1,0:T(8,128)(2,1)S(1)}, u32[]{:S(2)}, u32[]{:S(2)}) collective-permute-start(bf16[256,256]{1,0:T(8,128)(2,1)S(1)} %get-tuple-element.30), channel_id=1, source_target_pairs={{0,32},{4,36},{8,40},{12,44},{16,48},{20,52},{24,56},{28,60},{32,6... | collective-permute-start | bytes 393224 | tf_op jit(solution)/shard_map/ppermute | solution.py:37
  40.0 0.7 constant_dynamic-update-slice_fusion.5
  41.5 0.7 constant_dynamic-update-slice_fusion.3
  42.2 2.3 %collective-permute-done.7 = bf16[256,256]{1,0:T(8,128)(2,1)S(1)} collective-permute-done((bf16[256,256]{1,0:T(8,128)(2,1)S(1)}, bf16[256,256]{1,0:T(8,128)(2,1)S(1)}, u32[]{:S(2)}, u32[]{:S(2)}) %collective-permute-start.7) | collective-permute-done | bytes 131104 | tf_op jit(solution)/shard_map/ppermute | solution.py:37
  45.1 3.2 %fusion.30 = (f32[256,4]{0,1:T(4,128)S(1)}, f32[256,4,2304]{2,0,1:T(8,128)S(1)}) fusion(bf16[2304,256]{1,0:T(8,128)(2,1)} %constant_dynamic-update-slice_fusion.2, bf16[256,4,128]{0,2,1:T(8,128)(2,1)S(1)} %bitcast.35, pred[256]{0:T(512)(128)(4,1)S(1)} %compare_and_fusion, pred[256,2304]{1,0:T(8,128)(4,1)S(1)} %and_and_fusion), kind=kOutput, calls=%fused_computation.82 | convolution fusion | flops 611187712 | bytes 10883328 | tf_op jit(solution)/shard_map/bhd,td->bht/dot_general | solution.py:54
  48.3 1.4 %exponential_reduce_fusion = f32[256,4]{0,1:T(4,128)S(1)} fusion(f32[256,4,2304]{2,0,1:T(8,128)S(1)} %get-tuple-element.35, f32[256,4]{0,1:T(4,128)S(1)} %get-tuple-element.34), kind=kLoop, calls=%fused_computation.4 | loop fusion | flops 4717568 | bytes 9445376 | tf_op jit(solution)/shard_map/reduce_sum | solution.py:59
  49.7 2.2 %copy-done.1 = f32[256,4,2304]{2,0,1:T(8,128)} copy-done((f32[256,4,2304]{2,0,1:T(8,128)}, f32[256,4,2304]{2,0,1:T(8,128)S(1)}, u32[]{:S(2)}) %copy-start.1) | copy-done | bytes 9437208
  52.2 6.5 %multiply_reduce_fusion = (f32[256,4]{0,1:T(4,128)S(1)}, f32[256,4,128]{0,2,1:T(8,128)}) fusion(bf16[256,4,128]{0,2,1:T(8,128)(2,1)S(1)} %copy.38, bf16[2304,256]{1,0:T(8,128)(2,1)} %constant_dynamic-update-slice_fusion.2, f32[256,4,2304]{2,0,1:T(8,128)} %copy-done.1, f32[256,4]{0,1:T(4,128)S(1)} %log_add_fusion, pred[256,2304]{1,0:T(8,128)(4,1)S(1)} %and_and_fusion), kind=kOutput, calls=%fused_computation.31 | convolution fusion | flops 611712000 | bytes 11411456 | tf_op jit(solution)/shard_map/bht,td->bhd/dot_general | solution.py:62
  59.2 2.9 %fusion = bf16[256,4,2304]{2,0,1:T(8,128)(2,1)S(1)} fusion(f32[256,4,2304]{2,0,1:T(8,128)S(1)} %copy-done.2, bf16[256,4,128]{0,2,1:T(8,128)(2,1)S(1)} %copy.38, f32[256,4]{0,1:T(4,128)S(1)} %get-tuple-element.36, f32[256,4]{0,1:T(4,128)S(1)} %log_add_fusion, pred[256,2304]{1,0:T(8,128)(4,1)S(1)} %and_and_fusion, bf16[2304,256]{1,0:T(8,128)(2,1)S(1)} %copy-done.5), kind=kOutput, calls=%fused_computation.2 | convolution fusion | flops 615776256 | bytes 15605760 | tf_op jit(solution)/shard_map/bhd,td->bht/dot_general | solution.py:67
  62.2 1.4 %convolution_multiply_fusion = f32[256,4,128]{2,0,1:T(8,128)S(1)} fusion(bf16[256,4,2304]{2,0,1:T(8,128)(2,1)S(1)} %fusion, bf16[2304,256]{1,0:T(8,128)(2,1)S(1)} %copy-done.5), kind=kOutput, calls=%fused_computation.27 | convolution fusion | flops 604110848 | bytes 5832704 | tf_op jit(solution)/shard_map/bht,td->bhd/dot_general | solution.py:72
  63.6 0.8 fusion.2
  64.4 1.9 %convolution_bitcast_fusion = f32[2304,128]{0,1:T(8,128)S(1)} fusion(bf16[256,4,128]{0,2,1:T(8,128)(2,1)S(1)} %copy.38, f32[256,4,2304]{2,0,1:T(8,128)S(1)} %copy-done.2, f32[256,4]{0,1:T(4,128)S(1)} %log_add_fusion, pred[256,2304]{1,0:T(8,128)(4,1)S(1)} %and_and_fusion), kind=kOutput, calls=%fused_computation.23 | convolution fusion | flops 611057664 | bytes 11472896 | tf_op jit(solution)/shard_map/bht,bhd->td/dot_general | solution.py:79
  66.6 1.0 concatenate.20
  67.6 1.3 copy.36
  68.9 1.0 concatenate.19
  69.9 1.2 fusion.16
  71.2 3.2 %collective-permute-start.15 = (f32[256,256]{0,1:T(8,128)}, f32[256,256]{0,1:T(8,128)S(1)}, u32[]{:S(2)}, u32[]{:S(2)}) collective-permute-start(f32[256,256]{0,1:T(8,128)} %get-tuple-element.24), channel_id=1, source_target_pairs={{32,0},{36,4},{40,8},{44,12},{48,16},{52,20},{56,24},{60,28},{64,3... | collective-permute-start | bytes 786440 | tf_op jit(solution)/shard_map/ppermute | solution.py:85
  74.3 4.2 %collective-permute-start.14 = (f32[256,256]{0,1:T(8,128)}, f32[256,256]{0,1:T(8,128)S(1)}, u32[]{:S(2)}, u32[]{:S(2)}) collective-permute-start(f32[256,256]{0,1:T(8,128)} %get-tuple-element.25), channel_id=1, source_target_pairs={{28,0},{32,4},{36,8},{40,12},{44,16},{48,20},{52,24},{56,28},{60,3... | collective-permute-start | bytes 786440 | tf_op jit(solution)/shard_map/ppermute | solution.py:85
  78.5 2.0 %collective-permute-start.13 = (f32[256,256]{0,1:T(8,128)}, f32[256,256]{0,1:T(8,128)}, u32[]{:S(2)}, u32[]{:S(2)}) collective-permute-start(f32[256,256]{0,1:T(8,128)} %get-tuple-element.23), channel_id=1, source_target_pairs={{24,0},{28,4},{32,8},{36,12},{40,16},{44,20},{48,24},{52,28},{56,3... | collective-permute-start | bytes 786440 | tf_op jit(solution)/shard_map/ppermute | solution.py:85
  80.6 1.1 pad_maximum_fusion
  81.7 8.6 %all-to-all-start.1 = ((f32[32,8,1024]{2,1,0:T(8,128)}), f32[32,8,1024]{2,1,0:T(8,128)}, u32[]{:S(2)}, u32[]{:S(2)}) async-start(f32[32,8,1024]{2,1,0:T(8,128)} %pad_maximum_fusion), calls=%async_computation.1 | async-start | bytes 2097152 | tf_op jit(solution)/shard_map/all_to_all | solution.py:98
  90.3 3.3 %collective-permute-start.12 = (f32[256,256]{0,1:T(8,128)}, f32[256,256]{0,1:T(8,128)S(1)}, u32[]{:S(2)}, u32[]{:S(2)}) collective-permute-start(f32[256,256]{0,1:T(8,128)} %get-tuple-element.22), channel_id=1, source_target_pairs={{20,0},{24,4},{28,8},{32,12},{36,16},{40,20},{44,24},{48,28},{52,3... | collective-permute-start | bytes 786440 | tf_op jit(solution)/shard_map/ppermute | solution.py:85
  93.6 3.7 %collective-permute-start.11 = (f32[256,256]{0,1:T(8,128)}, f32[256,256]{0,1:T(8,128)S(1)}, u32[]{:S(2)}, u32[]{:S(2)}) collective-permute-start(f32[256,256]{0,1:T(8,128)} %get-tuple-element.21), channel_id=1, source_target_pairs={{16,0},{20,4},{24,8},{28,12},{32,16},{36,20},{40,24},{44,28},{48,3... | collective-permute-start | bytes 786440 | tf_op jit(solution)/shard_map/ppermute | solution.py:85
  97.4 1.9 %collective-permute-start.10 = (f32[256,256]{0,1:T(8,128)}, f32[256,256]{0,1:T(8,128)S(1)}, u32[]{:S(2)}, u32[]{:S(2)}) collective-permute-start(f32[256,256]{0,1:T(8,128)} %get-tuple-element.20), channel_id=1, source_target_pairs={{12,0},{16,4},{20,8},{24,12},{28,16},{32,20},{36,24},{40,28},{44,3... | collective-permute-start | bytes 786440 | tf_op jit(solution)/shard_map/ppermute | solution.py:85
  99.3 2.5 %collective-permute-start.9 = (f32[256,256]{0,1:T(8,128)}, f32[256,256]{0,1:T(8,128)S(1)}, u32[]{:S(2)}, u32[]{:S(2)}) collective-permute-start(f32[256,256]{0,1:T(8,128)} %get-tuple-element.19), channel_id=1, source_target_pairs={{8,0},{12,4},{16,8},{20,12},{24,16},{28,20},{32,24},{36,28},{40,32... | collective-permute-start | bytes 786440 | tf_op jit(solution)/shard_map/ppermute | solution.py:85
  101.8 2.9 %collective-permute-start.8 = (f32[256,256]{0,1:T(8,128)S(1)}, f32[256,256]{0,1:T(8,128)S(1)}, u32[]{:S(2)}, u32[]{:S(2)}) collective-permute-start(f32[256,256]{0,1:T(8,128)S(1)} %get-tuple-element.18), channel_id=1, source_target_pairs={{4,0},{8,4},{12,8},{16,12},{20,16},{24,20},{28,24},{32,28},{36,32}... | collective-permute-start | bytes 786440 | tf_op jit(solution)/shard_map/ppermute | solution.py:85
  104.7 3.0 %collective-permute-done.12 = f32[256,256]{0,1:T(8,128)S(1)} collective-permute-done((f32[256,256]{0,1:T(8,128)}, f32[256,256]{0,1:T(8,128)S(1)}, u32[]{:S(2)}, u32[]{:S(2)}) %collective-permute-start.12) | collective-permute-done | bytes 262176 | tf_op jit(solution)/shard_map/ppermute | solution.py:85
  107.7 7.6 %collective-permute-done.11 = f32[256,256]{0,1:T(8,128)S(1)} collective-permute-done((f32[256,256]{0,1:T(8,128)}, f32[256,256]{0,1:T(8,128)S(1)}, u32[]{:S(2)}, u32[]{:S(2)}) %collective-permute-start.11) | collective-permute-done | bytes 262176 | tf_op jit(solution)/shard_map/ppermute | solution.py:85
  115.3 4.5 %collective-permute-done.10 = f32[256,256]{0,1:T(8,128)S(1)} collective-permute-done((f32[256,256]{0,1:T(8,128)}, f32[256,256]{0,1:T(8,128)S(1)}, u32[]{:S(2)}, u32[]{:S(2)}) %collective-permute-start.10) | collective-permute-done | bytes 262176 | tf_op jit(solution)/shard_map/ppermute | solution.py:85
  119.8 7.9 %collective-permute-done.9 = f32[256,256]{0,1:T(8,128)S(1)} collective-permute-done((f32[256,256]{0,1:T(8,128)}, f32[256,256]{0,1:T(8,128)S(1)}, u32[]{:S(2)}, u32[]{:S(2)}) %collective-permute-start.9) | collective-permute-done | bytes 262176 | tf_op jit(solution)/shard_map/ppermute | solution.py:85
  127.7 4.0 %collective-permute-done.8 = f32[256,256]{0,1:T(8,128)S(1)} collective-permute-done((f32[256,256]{0,1:T(8,128)S(1)}, f32[256,256]{0,1:T(8,128)S(1)}, u32[]{:S(2)}, u32[]{:S(2)}) %collective-permute-start.8) | collective-permute-done | bytes 262176 | tf_op jit(solution)/shard_map/ppermute | solution.py:85
  131.7 1.1 fusion.15
  132.8 0.8 copy.42
  133.5 0.8 copy.43
  134.3 2.2 %fusion.28 = (f32[256,512]{1,0:T(8,128)}, f32[256,512]{1,0:T(8,128)}) fusion(f32[256,1024]{1,0:T(8,128)} %bitcast.10), kind=kLoop, calls=%fused_computation.80 | loop fusion | bytes 2097152 | tf_op jit(solution)/shard_map/slice | solution.py:100
  (46 shorter events, 6.4 us)
Async XLA Ops:
  0.6 28.3 %copy-start = (bf16[256,512]{1,0:T(8,128)(2,1)S(1)}, bf16[256,512]{1,0:T(8,128)(2,1)}, u32[]{:S(2)}) copy-start(bf16[256,512]{1,0:T(8,128)(2,1)} %param.6) | copy-start | bytes 786436
  3.7 26.5 %collective-permute-start = (bf16[256,256]{1,0:T(8,128)(2,1)S(1)}, bf16[256,256]{1,0:T(8,128)(2,1)S(1)}, u32[]{:S(2)}, u32[]{:S(2)}) collective-permute-start(bf16[256,256]{1,0:T(8,128)(2,1)S(1)} %get-tuple-element.30), channel_id=1, source_target_pairs={{0,4},{4,8},{8,12},{12,16},{16,20},{20,24},{24,28},{28,32},{32,36}... | collective-permute-start | bytes 393224 | tf_op jit(solution)/shard_map/ppermute | solution.py:37
  5.8 28.3 %collective-permute-start.1 = (bf16[256,256]{1,0:T(8,128)(2,1)S(1)}, bf16[256,256]{1,0:T(8,128)(2,1)S(1)}, u32[]{:S(2)}, u32[]{:S(2)}) collective-permute-start(bf16[256,256]{1,0:T(8,128)(2,1)S(1)} %get-tuple-element.30), channel_id=1, source_target_pairs={{0,8},{4,12},{8,16},{12,20},{16,24},{20,28},{24,32},{28,36},{32,40... | collective-permute-start | bytes 393224 | tf_op jit(solution)/shard_map/ppermute | solution.py:37
  9.3 27.3 %collective-permute-start.2 = (bf16[256,256]{1,0:T(8,128)(2,1)S(1)}, bf16[256,256]{1,0:T(8,128)(2,1)S(1)}, u32[]{:S(2)}, u32[]{:S(2)}) collective-permute-start(bf16[256,256]{1,0:T(8,128)(2,1)S(1)} %get-tuple-element.30), channel_id=1, source_target_pairs={{0,12},{4,16},{8,20},{12,24},{16,28},{20,32},{24,36},{28,40},{32,4... | collective-permute-start | bytes 393224 | tf_op jit(solution)/shard_map/ppermute | solution.py:37
  12.9 26.5 %collective-permute-start.3 = (bf16[256,256]{1,0:T(8,128)(2,1)S(1)}, bf16[256,256]{1,0:T(8,128)(2,1)S(1)}, u32[]{:S(2)}, u32[]{:S(2)}) collective-permute-start(bf16[256,256]{1,0:T(8,128)(2,1)S(1)} %get-tuple-element.30), channel_id=1, source_target_pairs={{0,16},{4,20},{8,24},{12,28},{16,32},{20,36},{24,40},{28,44},{32,4... | collective-permute-start | bytes 393224 | tf_op jit(solution)/shard_map/ppermute | solution.py:37
  15.9 24.2 %collective-permute-start.4 = (bf16[256,256]{1,0:T(8,128)(2,1)S(1)}, bf16[256,256]{1,0:T(8,128)(2,1)S(1)}, u32[]{:S(2)}, u32[]{:S(2)}) collective-permute-start(bf16[256,256]{1,0:T(8,128)(2,1)S(1)} %get-tuple-element.30), channel_id=1, source_target_pairs={{0,20},{4,24},{8,28},{12,32},{16,36},{20,40},{24,44},{28,48},{32,5... | collective-permute-start | bytes 393224 | tf_op jit(solution)/shard_map/ppermute | solution.py:37
  17.8 34.2 %all-to-all-start = ((bf16[32,8,512]{2,1,0:T(8,128)(2,1)}), bf16[32,8,512]{2,1,0:T(8,128)(2,1)S(1)}, u32[]{:S(2)}, u32[]{:S(2)}) async-start(bf16[32,8,512]{2,1,0:T(8,128)(2,1)} %bitcast.37), calls=%async_computation | async-start | bytes 524288 | tf_op jit(solution)/shard_map/all_to_all | solution.py:30
  30.2 10.5 %collective-permute-start.5 = (bf16[256,256]{1,0:T(8,128)(2,1)S(1)}, bf16[256,256]{1,0:T(8,128)(2,1)S(1)}, u32[]{:S(2)}, u32[]{:S(2)}) collective-permute-start(bf16[256,256]{1,0:T(8,128)(2,1)S(1)} %get-tuple-element.30), channel_id=1, source_target_pairs={{0,24},{4,28},{8,32},{12,36},{16,40},{20,44},{24,48},{28,52},{32,5... | collective-permute-start | bytes 393224 | tf_op jit(solution)/shard_map/ppermute | solution.py:37
  34.0 7.5 %collective-permute-start.6 = (bf16[256,256]{1,0:T(8,128)(2,1)S(1)}, bf16[256,256]{1,0:T(8,128)(2,1)S(1)}, u32[]{:S(2)}, u32[]{:S(2)}) collective-permute-start(bf16[256,256]{1,0:T(8,128)(2,1)S(1)} %get-tuple-element.30), channel_id=1, source_target_pairs={{0,28},{4,32},{8,36},{12,40},{16,44},{20,48},{24,52},{28,56},{32,6... | collective-permute-start | bytes 393224 | tf_op jit(solution)/shard_map/ppermute | solution.py:37
  36.6 7.8 %collective-permute-start.7 = (bf16[256,256]{1,0:T(8,128)(2,1)S(1)}, bf16[256,256]{1,0:T(8,128)(2,1)S(1)}, u32[]{:S(2)}, u32[]{:S(2)}) collective-permute-start(bf16[256,256]{1,0:T(8,128)(2,1)S(1)} %get-tuple-element.30), channel_id=1, source_target_pairs={{0,32},{4,36},{8,40},{12,44},{16,48},{20,52},{24,56},{28,60},{32,6... | collective-permute-start | bytes 393224 | tf_op jit(solution)/shard_map/ppermute | solution.py:37
  48.3 3.7 %copy-start.1 = (f32[256,4,2304]{2,0,1:T(8,128)}, f32[256,4,2304]{2,0,1:T(8,128)S(1)}, u32[]{:S(2)}) copy-start(f32[256,4,2304]{2,0,1:T(8,128)S(1)} %get-tuple-element.35) | copy-start | bytes 28311556
  52.2 6.5 %copy-start.2 = (f32[256,4,2304]{2,0,1:T(8,128)S(1)}, f32[256,4,2304]{2,0,1:T(8,128)}, u32[]{:S(2)}) copy-start(f32[256,4,2304]{2,0,1:T(8,128)} %copy-done.1) | copy-start | bytes 28311556
  52.2 7.0 %copy-start.5 = (bf16[2304,256]{1,0:T(8,128)(2,1)S(1)}, bf16[2304,256]{1,0:T(8,128)(2,1)}, u32[]{:S(2)}) copy-start(bf16[2304,256]{1,0:T(8,128)(2,1)} %constant_dynamic-update-slice_fusion.2) | copy-start | bytes 3538948
  69.9 10.6 %copy-start.3 = (f32[32,8,512]{2,1,0:T(8,128)S(1)}, f32[32,8,512]{2,1,0:T(8,128)}, u32[]{:S(2)}) copy-start(f32[32,8,512]{2,1,0:T(8,128)} %concatenate.20) | copy-start | bytes 1572868
  69.9 10.6 %copy-start.4 = (f32[32,8,512]{2,1,0:T(8,128)S(1)}, f32[32,8,512]{2,1,0:T(8,128)}, u32[]{:S(2)}) copy-start(f32[32,8,512]{2,1,0:T(8,128)} %concatenate.19) | copy-start | bytes 1572868
  71.2 26.2 %collective-permute-start.15 = (f32[256,256]{0,1:T(8,128)}, f32[256,256]{0,1:T(8,128)S(1)}, u32[]{:S(2)}, u32[]{:S(2)}) collective-permute-start(f32[256,256]{0,1:T(8,128)} %get-tuple-element.24), channel_id=1, source_target_pairs={{32,0},{36,4},{40,8},{44,12},{48,16},{52,20},{56,24},{60,28},{64,3... | collective-permute-start | bytes 786440 | tf_op jit(solution)/shard_map/ppermute | solution.py:85
  74.3 25.0 %collective-permute-start.14 = (f32[256,256]{0,1:T(8,128)}, f32[256,256]{0,1:T(8,128)S(1)}, u32[]{:S(2)}, u32[]{:S(2)}) collective-permute-start(f32[256,256]{0,1:T(8,128)} %get-tuple-element.25), channel_id=1, source_target_pairs={{28,0},{32,4},{36,8},{40,12},{44,16},{48,20},{52,24},{56,28},{60,3... | collective-permute-start | bytes 786440 | tf_op jit(solution)/shard_map/ppermute | solution.py:85
  78.5 23.2 %collective-permute-start.13 = (f32[256,256]{0,1:T(8,128)}, f32[256,256]{0,1:T(8,128)}, u32[]{:S(2)}, u32[]{:S(2)}) collective-permute-start(f32[256,256]{0,1:T(8,128)} %get-tuple-element.23), channel_id=1, source_target_pairs={{24,0},{28,4},{32,8},{36,12},{40,16},{44,20},{48,24},{52,28},{56,3... | collective-permute-start | bytes 786440 | tf_op jit(solution)/shard_map/ppermute | solution.py:85
  81.7 52.6 %all-to-all-start.1 = ((f32[32,8,1024]{2,1,0:T(8,128)}), f32[32,8,1024]{2,1,0:T(8,128)}, u32[]{:S(2)}, u32[]{:S(2)}) async-start(f32[32,8,1024]{2,1,0:T(8,128)} %pad_maximum_fusion), calls=%async_computation.1 | async-start | bytes 2097152 | tf_op jit(solution)/shard_map/all_to_all | solution.py:98
  90.3 17.4 %collective-permute-start.12 = (f32[256,256]{0,1:T(8,128)}, f32[256,256]{0,1:T(8,128)S(1)}, u32[]{:S(2)}, u32[]{:S(2)}) collective-permute-start(f32[256,256]{0,1:T(8,128)} %get-tuple-element.22), channel_id=1, source_target_pairs={{20,0},{24,4},{28,8},{32,12},{36,16},{40,20},{44,24},{48,28},{52,3... | collective-permute-start | bytes 786440 | tf_op jit(solution)/shard_map/ppermute | solution.py:85
  93.6 21.7 %collective-permute-start.11 = (f32[256,256]{0,1:T(8,128)}, f32[256,256]{0,1:T(8,128)S(1)}, u32[]{:S(2)}, u32[]{:S(2)}) collective-permute-start(f32[256,256]{0,1:T(8,128)} %get-tuple-element.21), channel_id=1, source_target_pairs={{16,0},{20,4},{24,8},{28,12},{32,16},{36,20},{40,24},{44,28},{48,3... | collective-permute-start | bytes 786440 | tf_op jit(solution)/shard_map/ppermute | solution.py:85
  97.4 22.5 %collective-permute-start.10 = (f32[256,256]{0,1:T(8,128)}, f32[256,256]{0,1:T(8,128)S(1)}, u32[]{:S(2)}, u32[]{:S(2)}) collective-permute-start(f32[256,256]{0,1:T(8,128)} %get-tuple-element.20), channel_id=1, source_target_pairs={{12,0},{16,4},{20,8},{24,12},{28,16},{32,20},{36,24},{40,28},{44,3... | collective-permute-start | bytes 786440 | tf_op jit(solution)/shard_map/ppermute | solution.py:85
  99.3 28.4 %collective-permute-start.9 = (f32[256,256]{0,1:T(8,128)}, f32[256,256]{0,1:T(8,128)S(1)}, u32[]{:S(2)}, u32[]{:S(2)}) collective-permute-start(f32[256,256]{0,1:T(8,128)} %get-tuple-element.19), channel_id=1, source_target_pairs={{8,0},{12,4},{16,8},{20,12},{24,16},{28,20},{32,24},{36,28},{40,32... | collective-permute-start | bytes 786440 | tf_op jit(solution)/shard_map/ppermute | solution.py:85
  101.8 29.9 %collective-permute-start.8 = (f32[256,256]{0,1:T(8,128)S(1)}, f32[256,256]{0,1:T(8,128)S(1)}, u32[]{:S(2)}, u32[]{:S(2)}) collective-permute-start(f32[256,256]{0,1:T(8,128)S(1)} %get-tuple-element.18), channel_id=1, source_target_pairs={{4,0},{8,4},{12,8},{16,12},{20,16},{24,20},{28,24},{32,28},{36,32}... | collective-permute-start | bytes 786440 | tf_op jit(solution)/shard_map/ppermute | solution.py:85

commit v2 on v1

--- a/solution.py
+++ b/solution.py
@@ -72,32 +72,40 @@
         jnp.einsum("bht,td->bhd", score_grads, key_all, preferred_element_type=jnp.float32)
         * score_scale
     )
-    key_term = (
-        jnp.einsum("bht,bhd->td", score_grads, query_heads, preferred_element_type=jnp.float32)
-        * score_scale
+    width = head_count * head_dim
+    attended_out = lax.all_to_all(
+        attended.reshape(tok_rows, width), "seq", 0, 0, tiled=True
     )
-    value_term = jnp.einsum(
-        "bht,bhd->td", weights_low, grad_heads, preferred_element_type=jnp.float32
-    )
-    terms = jnp.concatenate([key_term, value_term], axis=1).reshape(halo + 1, tok_rows, -1)
-    total = terms[0]
-    for shift in range(1, halo + 1):
-        total = total + lax.ppermute(
-            terms[shift], "seq", [(i, i - shift) for i in range(shift, shard_count)]
+
+    def block_terms(shift):
+        cols = slice(shift * tok_rows, (shift + 1) * tok_rows)
+        key_term = (
+            jnp.einsum(
+                "bht,bhd->td",
+                score_grads[:, :, cols],
+                query_heads,
+                preferred_element_type=jnp.float32,
+            )
+            * score_scale
         )
+        value_term = jnp.einsum(
+            "bht,bhd->td", weights_low[:, :, cols], grad_heads, preferred_element_type=jnp.float32
+        )
+        return jnp.concatenate([key_term, value_term], axis=1)
+
+    arrived = []
+    for shift in range(halo, 0, -1):
+        sent = block_terms(shift).astype(jnp.bfloat16)
+        arrived.append(
+            lax.ppermute(sent, "seq", [(i, i - shift) for i in range(shift, shard_count)])
+        )
+    total = block_terms(0)
+    for part in arrived:
+        total = total + part.astype(jnp.float32)
     key_grad = total[:, :head_dim]
     value_grad = total[:, head_dim:]
-
-    row_outs = jnp.concatenate(
-        [
-            attended.reshape(tok_rows, head_count * head_dim),
-            grad_query.reshape(tok_rows, head_count * head_dim),
-        ],
-        axis=1,
-    )
-    balanced = lax.all_to_all(row_outs, "seq", 0, 0, tiled=True)
-    width = head_count * head_dim
-    return (balanced[:, :width], balanced[:, width:], key_grad, value_grad)
+    query_out = lax.all_to_all(grad_query.reshape(tok_rows, width), "seq", 0, 0, tiled=True)
+    return (attended_out, query_out, key_grad, value_grad)
 
 
 def solution(mesh):

time: 137 us -> 139 us (1.015)
  the two profiles are of different devices: /device:TPU:119 before, /device:TPU:1 now
where the time goes in v2:
time: 139 us; the launch traced here: 137 us
  starting transfers between devices  69.2 us (50%)
  matrix products  27.4 us (20%)
  waiting for transfers between devices  16.3 us (12%)
  local copies, waits for them, and re-layouts  13.3 us (10%)
  other arithmetic  9.73 us (7%)
    ppermute x8, starting transfers between devices, per_device(): lax.ppermute(pair, 'seq', [(i, i + shift) for i in range(shard_count - sh...  31.3 us
    all_to_all x1, starting transfers between devices, per_device(): lax.all_to_all(attended.reshape(tok_rows, width), 'seq', 0, 0, tiled=True)  13.2 us
    dot_general x9, matrix products, block_terms(): jnp.einsum('bht,bhd->td', weights_low[:, :, cols], grad_heads, preferred_...  13.2 us
    ppermute x8, starting transfers between devices, per_device(): lax.ppermute(sent, 'seq', [(i, i - shift) for i in range(shift, shard_cou...  10.9 us
    all_to_all x1, starting transfers between devices, per_device(): lax.all_to_all(grad_query.reshape(tok_rows, width), 'seq', 0, 0, tiled=True)  7.98 us
    all_to_all x1, waiting for transfers between devices, per_device(): lax.all_to_all(attended.reshape(tok_rows, width), 'seq', 0, 0, tiled=True)  7.61 us
    unnamed x24, local copies, waits for them, and re-layouts  6.95 us
    all_to_all x1, starting transfers between devices, per_device(): grad_rows = lax.all_to_all(grad_out, 'seq', 0, 0, tiled=True)  5.79 us
  transfers between devices with their start and end apart: 19, of which 4 were waited for; matrix products, arithmetic and copies ran while one was open for 13% of the time, Pallas kernels for 0%

profile of v2, /device:TPU:1, one launch (start us, length us, event | category | flops | bytes accessed | tf_op | source)
XLA Modules:
  0.0 137.3 jit_solution(11111791254773707089)
XLA Ops:
  0.6 1.5 %constant_dynamic-update-slice_fusion.1 = (bf16[256,256]{1,0:T(8,128)(2,1)}, bf16[2304,256]{1,0:T(8,128)(2,1)S(1)}) fusion(bf16[256,128]{1,0:T(8,128)(2,1)} %param.7), kind=kLoop, calls=%fused_computation.93 | loop fusion | bytes 196608
  2.2 1.5 %constant_dynamic-update-slice_fusion = (bf16[256,256]{1,0:T(8,128)(2,1)}, bf16[2304,256]{1,0:T(8,128)(2,1)S(1)}) fusion(bf16[256,256]{1,0:T(8,128)(2,1)} %get-tuple-element.22, bf16[256,128]{1,0:T(8,128)(2,1)} %param.8, bf16[2304,256]{1,0:T(8,128)(2,1)S(1)} %get-tuple-element.23), kind=kLoop, calls=%fused_computation.92 | loop fusion | bytes 196608 | tf_op jit(solution)/shard_map/concatenate | solution.py:33
  3.7 4.0 %collective-permute-start.7 = (bf16[256,256]{1,0:T(8,128)(2,1)}, bf16[256,256]{1,0:T(8,128)(2,1)S(1)}, u32[]{:S(2)}, u32[]{:S(2)}) collective-permute-start(bf16[256,256]{1,0:T(8,128)(2,1)} %get-tuple-element.20), channel_id=1, source_target_pairs={{0,32},{4,36},{8,40},{12,44},{16,48},{20,52},{24,56},{28,60},{32,6... | collective-permute-start | bytes 393224 | tf_op jit(solution)/shard_map/ppermute | solution.py:37
  7.7 4.0 %collective-permute-start.6 = (bf16[256,256]{1,0:T(8,128)(2,1)}, bf16[256,256]{1,0:T(8,128)(2,1)S(1)}, u32[]{:S(2)}, u32[]{:S(2)}) collective-permute-start(bf16[256,256]{1,0:T(8,128)(2,1)} %get-tuple-element.20), channel_id=1, source_target_pairs={{0,28},{4,32},{8,36},{12,40},{16,44},{20,48},{24,52},{28,56},{32,6... | collective-permute-start | bytes 393224 | tf_op jit(solution)/shard_map/ppermute | solution.py:37
  11.7 5.7 %collective-permute-start.5 = (bf16[256,256]{1,0:T(8,128)(2,1)}, bf16[256,256]{1,0:T(8,128)(2,1)S(1)}, u32[]{:S(2)}, u32[]{:S(2)}) collective-permute-start(bf16[256,256]{1,0:T(8,128)(2,1)} %get-tuple-element.20), channel_id=1, source_target_pairs={{0,24},{4,28},{8,32},{12,36},{16,40},{20,44},{24,48},{28,52},{32,5... | collective-permute-start | bytes 393224 | tf_op jit(solution)/shard_map/ppermute | solution.py:37
  17.4 1.3 collective-permute-start.1
  18.7 3.4 %collective-permute-start = (bf16[256,256]{1,0:T(8,128)(2,1)}, bf16[256,256]{1,0:T(8,128)(2,1)S(1)}, u32[]{:S(2)}, u32[]{:S(2)}) collective-permute-start(bf16[256,256]{1,0:T(8,128)(2,1)} %get-tuple-element.20), channel_id=1, source_target_pairs={{0,4},{4,8},{8,12},{12,16},{16,20},{20,24},{24,28},{28,32},{32,36}... | collective-permute-start | bytes 393224 | tf_op jit(solution)/shard_map/ppermute | solution.py:37
  22.2 5.8 %all-to-all-start.1 = ((bf16[32,8,512]{2,1,0:T(8,128)(2,1)}), bf16[32,8,512]{2,1,0:T(8,128)(2,1)S(1)}, u32[]{:S(2)}, u32[]{:S(2)}) async-start(bf16[32,8,512]{2,1,0:T(8,128)(2,1)} %bitcast.126), calls=%async_computation.1 | async-start | bytes 524288 | tf_op jit(solution)/shard_map/all_to_all | solution.py:30
  30.5 1.2 gather_fusion
  31.8 5.0 %collective-permute-start.2 = (bf16[256,256]{1,0:T(8,128)(2,1)}, bf16[256,256]{1,0:T(8,128)(2,1)S(1)}, u32[]{:S(2)}, u32[]{:S(2)}) collective-permute-start(bf16[256,256]{1,0:T(8,128)(2,1)} %get-tuple-element.20), channel_id=1, source_target_pairs={{0,12},{4,16},{8,20},{12,24},{16,28},{20,32},{24,36},{28,40},{32,4... | collective-permute-start | bytes 393224 | tf_op jit(solution)/shard_map/ppermute | solution.py:37
  36.9 3.1 %collective-permute-start.3 = (bf16[256,256]{1,0:T(8,128)(2,1)}, bf16[256,256]{1,0:T(8,128)(2,1)S(1)}, u32[]{:S(2)}, u32[]{:S(2)}) collective-permute-start(bf16[256,256]{1,0:T(8,128)(2,1)} %get-tuple-element.20), channel_id=1, source_target_pairs={{0,16},{4,20},{8,24},{12,28},{16,32},{20,36},{24,40},{28,44},{32,4... | collective-permute-start | bytes 393224 | tf_op jit(solution)/shard_map/ppermute | solution.py:37
  40.0 4.7 %collective-permute-start.4 = (bf16[256,256]{1,0:T(8,128)(2,1)}, bf16[256,256]{1,0:T(8,128)(2,1)S(1)}, u32[]{:S(2)}, u32[]{:S(2)}) collective-permute-start(bf16[256,256]{1,0:T(8,128)(2,1)} %get-tuple-element.20), channel_id=1, source_target_pairs={{0,20},{4,24},{8,28},{12,32},{16,36},{20,40},{24,44},{28,48},{32,5... | collective-permute-start | bytes 393224 | tf_op jit(solution)/shard_map/ppermute | solution.py:37
  44.8 3.4 %collective-permute-done.4 = bf16[256,256]{1,0:T(8,128)(2,1)S(1)} collective-permute-done((bf16[256,256]{1,0:T(8,128)(2,1)}, bf16[256,256]{1,0:T(8,128)(2,1)S(1)}, u32[]{:S(2)}, u32[]{:S(2)}) %collective-permute-start.4) | collective-permute-done | bytes 131104 | tf_op jit(solution)/shard_map/ppermute | solution.py:37
  48.3 2.1 %fusion.54 = (f32[256,4]{0,1:T(4,128)S(1)}, f32[256,4,2304]{2,0,1:T(8,128)S(1)}) fusion(bf16[2304,256]{1,0:T(8,128)(2,1)S(1)} %constant_dynamic-update-slice_fusion.2, bf16[256,4,128]{0,2,1:T(8,128)(2,1)S(1)} %bitcast.127, pred[256]{0:T(512)(128)(4,1)S(1)} %compare_and_fusion, pred[256,2304]{1,0:T(8,128)(4,1)S(1)} %and_and_fusion), kind=kOutput, calls=%fused_computation.115 | convolution fusion | flops 611187712 | bytes 10883584 | tf_op jit(solution)/shard_map/bhd,td->bht/dot_general | solution.py:54
  50.4 1.4 %exponential_reduce_fusion = f32[256,4]{0,1:T(4,128)S(1)} fusion(f32[256,4,2304]{2,0,1:T(8,128)S(1)} %get-tuple-element.25, f32[256,4]{0,1:T(4,128)S(1)} %get-tuple-element.24), kind=kLoop, calls=%fused_computation.4 | loop fusion | flops 4717568 | bytes 9445376 | tf_op jit(solution)/shard_map/reduce_sum | solution.py:59
  51.8 2.2 %copy-done.1 = f32[256,4,2304]{2,0,1:T(8,128)} copy-done((f32[256,4,2304]{2,0,1:T(8,128)}, f32[256,4,2304]{2,0,1:T(8,128)S(1)}, u32[]{:S(2)}) %copy-start.1) | copy-done | bytes 9437208
  54.1 3.9 %fusion.1 = bf16[256,4,2304]{2,0,1:T(8,128)(2,1)} fusion(f32[256,4,2304]{2,0,1:T(8,128)S(1)} %get-tuple-element.25, f32[256,4]{0,1:T(4,128)S(1)} %log_add_fusion, pred[256,2304]{1,0:T(8,128)(4,1)S(1)} %and_and_fusion), kind=kLoop, calls=%fused_computation.6 | loop fusion | flops 7077888 | bytes 14749696 | tf_op jit(solution)/shard_map/convert_element_type | solution.py:61
  58.2 1.9 %fusion.26 = bf16[256,128]{0,1:T(8,128)(2,1)} fusion(bf16[256,4,128]{0,2,1:T(8,128)(2,1)S(1)} %copy.46, bf16[256,4,2304]{2,0,1:T(8,128)(2,1)} %fusion.1), kind=kOutput, calls=%fused_computation.51 | convolution fusion | flops 67141632 | bytes 851968 | tf_op jit(solution)/shard_map/bht,bhd->td/dot_general | solution.py:91
  60.1 1.9 %fusion.25 = bf16[256,128]{0,1:T(8,128)(2,1)} fusion(bf16[256,4,128]{0,2,1:T(8,128)(2,1)S(1)} %copy.46, bf16[256,4,2304]{2,0,1:T(8,128)(2,1)} %fusion.1), kind=kOutput, calls=%fused_computation.50 | convolution fusion | flops 67141632 | bytes 851968 | tf_op jit(solution)/shard_map/bht,bhd->td/dot_general | solution.py:91
  62.0 1.3 fusion.24
  63.3 1.3 fusion.23
  64.6 1.4 %fusion.22 = bf16[256,128]{0,1:T(8,128)(2,1)S(1)} fusion(bf16[256,4,128]{0,2,1:T(8,128)(2,1)S(1)} %copy.46, bf16[256,4,2304]{2,0,1:T(8,128)(2,1)} %fusion.1), kind=kOutput, calls=%fused_computation.47 | convolution fusion | flops 67141632 | bytes 851968 | tf_op jit(solution)/shard_map/bht,bhd->td/dot_general | solution.py:91
  66.0 1.6 %fusion.21 = bf16[256,128]{0,1:T(8,128)(2,1)S(1)} fusion(bf16[256,4,128]{0,2,1:T(8,128)(2,1)S(1)} %copy.46, bf16[256,4,2304]{2,0,1:T(8,128)(2,1)} %fusion.1), kind=kOutput, calls=%fused_computation.46 | convolution fusion | flops 67141632 | bytes 851968 | tf_op jit(solution)/shard_map/bht,bhd->td/dot_general | solution.py:91
  67.6 1.3 fusion.20
  68.9 1.3 fusion.19
  70.1 4.0 %multiply_reduce_fusion = (f32[256,4]{0,1:T(4,128)S(1)}, f32[256,4,128]{0,2,1:T(8,128)S(1)}) fusion(bf16[256,4,128]{0,2,1:T(8,128)(2,1)S(1)} %copy.46, bf16[256,4,2304]{2,0,1:T(8,128)(2,1)} %fusion.1, bf16[2304,256]{1,0:T(8,128)(2,1)S(1)} %constant_dynamic-update-slice_fusion.2), kind=kOutput, calls=%fused_computation.72 | convolution fusion | flops 604634112 | bytes 6098944 | tf_op jit(solution)/shard_map/bht,td->bhd/dot_general | solution.py:62
  74.2 2.9 %fusion = bf16[256,4,2304]{2,0,1:T(8,128)(2,1)S(1)} fusion(f32[256,4,2304]{2,0,1:T(8,128)S(1)} %copy-done.2, bf16[256,4,128]{0,2,1:T(8,128)(2,1)S(1)} %copy.46, f32[256,4]{0,1:T(4,128)S(1)} %get-tuple-element.26, f32[256,4]{0,1:T(4,128)S(1)} %log_add_fusion, pred[256,2304]{1,0:T(8,128)(4,1)S(1)} %and_and_fusion, ...), kind=kOutput, calls=%fused_computation.2 | convolution fusion | flops 615776256 | bytes 15605760 | tf_op jit(solution)/shard_map/bhd,td->bht/dot_general | solution.py:67
  77.2 1.4 %convolution_multiply_fusion = f32[256,4,128]{2,0,1:T(8,128)S(1)} fusion(bf16[256,4,2304]{2,0,1:T(8,128)(2,1)S(1)} %fusion, bf16[2304,256]{1,0:T(8,128)(2,1)S(1)} %constant_dynamic-update-slice_fusion.2), kind=kOutput, calls=%fused_computation.8 | convolution fusion | flops 604110848 | bytes 5832704 | tf_op jit(solution)/shard_map/bht,td->bhd/dot_general | solution.py:72
  79.0 0.9 fusion.13
  81.5 1.0 all_to_all.27
  82.5 8.0 %all-to-all-start.2 = ((f32[32,8,512]{2,1,0:T(8,128)}), f32[32,8,512]{2,1,0:T(8,128)S(1)}, u32[]{:S(2)}, u32[]{:S(2)}) async-start(f32[32,8,512]{2,1,0:T(8,128)} %all_to_all.27), calls=%async_computation.2 | async-start | bytes 1048576 | tf_op jit(solution)/shard_map/all_to_all | solution.py:107
  90.5 1.3 collective-permute-start.8
  91.8 1.3 collective-permute-start.9
  93.1 1.3 collective-permute-start.10
  94.5 1.3 collective-permute-start.11
  95.8 1.3 collective-permute-start.12
  97.1 1.3 fusion.2
  99.3 1.0 all_to_all.22
  100.3 0.8 pad_maximum_fusion.5
  101.2 1.3 collective-permute-start.13
  102.5 2.6 %collective-permute-done.9 = bf16[256,256]{0,1:T(8,128)(2,1)S(1)} collective-permute-done((bf16[256,256]{0,1:T(8,128)(2,1)S(1)}, bf16[256,256]{0,1:T(8,128)(2,1)S(1)}, u32[]{:S(2)}, u32[]{:S(2)}) %collective-permute-start.9) | collective-permute-done | bytes 131104 | tf_op jit(solution)/shard_map/ppermute | solution.py:100
  105.1 1.3 collective-permute-start.14
  106.4 2.6 %collective-permute-done.10 = bf16[256,256]{0,1:T(8,128)(2,1)S(1)} collective-permute-done((bf16[256,256]{0,1:T(8,128)(2,1)S(1)}, bf16[256,256]{0,1:T(8,128)(2,1)S(1)}, u32[]{:S(2)}, u32[]{:S(2)}) %collective-permute-start.10) | collective-permute-done | bytes 131104 | tf_op jit(solution)/shard_map/ppermute | solution.py:100
  109.0 1.9 %collective-permute-start.15 = (bf16[256,256]{0,1:T(8,128)(2,1)S(1)}, bf16[256,256]{0,1:T(8,128)(2,1)S(1)}, u32[]{:S(2)}, u32[]{:S(2)}) collective-permute-start(bf16[256,256]{0,1:T(8,128)(2,1)S(1)} %pad_maximum_fusion.7), channel_id=1, source_target_pairs={{4,0},{8,4},{12,8},{16,12},{20,16},{24,20},{28,24},{32,28},{36,32}... | collective-permute-start | bytes 393224 | tf_op jit(solution)/shard_map/ppermute | solution.py:100
  110.9 13.2 %all-to-all-start = ((f32[32,8,512]{2,1,0:T(8,128)}), f32[32,8,512]{2,1,0:T(8,128)S(1)}, u32[]{:S(2)}, u32[]{:S(2)}) async-start(f32[32,8,512]{2,1,0:T(8,128)} %all_to_all.22), calls=%async_computation | async-start | bytes 1048576 | tf_op jit(solution)/shard_map/all_to_all | solution.py:76
  124.2 1.3 convolution_bitcast_fusion.16
  125.5 1.1 fusion.52
  128.1 7.6 %all-to-all-done = f32[32,8,512]{2,1,0:T(8,128)S(1)} async-done(((f32[32,8,512]{2,1,0:T(8,128)}), f32[32,8,512]{2,1,0:T(8,128)S(1)}, u32[]{:S(2)}, u32[]{:S(2)}) %all-to-all-start) | async-done | bytes 524320 | tf_op jit(solution)/shard_map/all_to_all | solution.py:76
  (72 shorter events, 9.1 us)
Async XLA Ops:
  0.6 29.9 %copy-start = (bf16[256,512]{1,0:T(8,128)(2,1)S(1)}, bf16[256,512]{1,0:T(8,128)(2,1)}, u32[]{:S(2)}) copy-start(bf16[256,512]{1,0:T(8,128)(2,1)} %param.6) | copy-start | bytes 786436
  3.7 44.6 %collective-permute-start.7 = (bf16[256,256]{1,0:T(8,128)(2,1)}, bf16[256,256]{1,0:T(8,128)(2,1)S(1)}, u32[]{:S(2)}, u32[]{:S(2)}) collective-permute-start(bf16[256,256]{1,0:T(8,128)(2,1)} %get-tuple-element.20), channel_id=1, source_target_pairs={{0,32},{4,36},{8,40},{12,44},{16,48},{20,52},{24,56},{28,60},{32,6... | collective-permute-start | bytes 393224 | tf_op jit(solution)/shard_map/ppermute | solution.py:37
  7.7 40.5 %collective-permute-start.6 = (bf16[256,256]{1,0:T(8,128)(2,1)}, bf16[256,256]{1,0:T(8,128)(2,1)S(1)}, u32[]{:S(2)}, u32[]{:S(2)}) collective-permute-start(bf16[256,256]{1,0:T(8,128)(2,1)} %get-tuple-element.20), channel_id=1, source_target_pairs={{0,28},{4,32},{8,36},{12,40},{16,44},{20,48},{24,52},{28,56},{32,6... | collective-permute-start | bytes 393224 | tf_op jit(solution)/shard_map/ppermute | solution.py:37
  11.7 36.5 %collective-permute-start.5 = (bf16[256,256]{1,0:T(8,128)(2,1)}, bf16[256,256]{1,0:T(8,128)(2,1)S(1)}, u32[]{:S(2)}, u32[]{:S(2)}) collective-permute-start(bf16[256,256]{1,0:T(8,128)(2,1)} %get-tuple-element.20), channel_id=1, source_target_pairs={{0,24},{4,28},{8,32},{12,36},{16,40},{20,44},{24,48},{28,52},{32,5... | collective-permute-start | bytes 393224 | tf_op jit(solution)/shard_map/ppermute | solution.py:37
  17.4 19.5 %collective-permute-start.1 = (bf16[256,256]{1,0:T(8,128)(2,1)}, bf16[256,256]{1,0:T(8,128)(2,1)S(1)}, u32[]{:S(2)}, u32[]{:S(2)}) collective-permute-start(bf16[256,256]{1,0:T(8,128)(2,1)} %get-tuple-element.20), channel_id=1, source_target_pairs={{0,8},{4,12},{8,16},{12,20},{16,24},{20,28},{24,32},{28,36},{32,40... | collective-permute-start | bytes 393224 | tf_op jit(solution)/shard_map/ppermute | solution.py:37
  18.7 13.1 %collective-permute-start = (bf16[256,256]{1,0:T(8,128)(2,1)}, bf16[256,256]{1,0:T(8,128)(2,1)S(1)}, u32[]{:S(2)}, u32[]{:S(2)}) collective-permute-start(bf16[256,256]{1,0:T(8,128)(2,1)} %get-tuple-element.20), channel_id=1, source_target_pairs={{0,4},{4,8},{8,12},{12,16},{16,20},{20,24},{24,28},{28,32},{32,36}... | collective-permute-start | bytes 393224 | tf_op jit(solution)/shard_map/ppermute | solution.py:37
  22.2 35.8 %all-to-all-start.1 = ((bf16[32,8,512]{2,1,0:T(8,128)(2,1)}), bf16[32,8,512]{2,1,0:T(8,128)(2,1)S(1)}, u32[]{:S(2)}, u32[]{:S(2)}) async-start(bf16[32,8,512]{2,1,0:T(8,128)(2,1)} %bitcast.126), calls=%async_computation.1 | async-start | bytes 524288 | tf_op jit(solution)/shard_map/all_to_all | solution.py:30
  31.8 8.2 %collective-permute-start.2 = (bf16[256,256]{1,0:T(8,128)(2,1)}, bf16[256,256]{1,0:T(8,128)(2,1)S(1)}, u32[]{:S(2)}, u32[]{:S(2)}) collective-permute-start(bf16[256,256]{1,0:T(8,128)(2,1)} %get-tuple-element.20), channel_id=1, source_target_pairs={{0,12},{4,16},{8,20},{12,24},{16,28},{20,32},{24,36},{28,40},{32,4... | collective-permute-start | bytes 393224 | tf_op jit(solution)/shard_map/ppermute | solution.py:37
  36.9 7.9 %collective-permute-start.3 = (bf16[256,256]{1,0:T(8,128)(2,1)}, bf16[256,256]{1,0:T(8,128)(2,1)S(1)}, u32[]{:S(2)}, u32[]{:S(2)}) collective-permute-start(bf16[256,256]{1,0:T(8,128)(2,1)} %get-tuple-element.20), channel_id=1, source_target_pairs={{0,16},{4,20},{8,24},{12,28},{16,32},{20,36},{24,40},{28,44},{32,4... | collective-permute-start | bytes 393224 | tf_op jit(solution)/shard_map/ppermute | solution.py:37
  40.0 8.2 %collective-permute-start.4 = (bf16[256,256]{1,0:T(8,128)(2,1)}, bf16[256,256]{1,0:T(8,128)(2,1)S(1)}, u32[]{:S(2)}, u32[]{:S(2)}) collective-permute-start(bf16[256,256]{1,0:T(8,128)(2,1)} %get-tuple-element.20), channel_id=1, source_target_pairs={{0,20},{4,24},{8,28},{12,32},{16,36},{20,40},{24,44},{28,48},{32,5... | collective-permute-start | bytes 393224 | tf_op jit(solution)/shard_map/ppermute | solution.py:37
  50.4 3.7 %copy-start.1 = (f32[256,4,2304]{2,0,1:T(8,128)}, f32[256,4,2304]{2,0,1:T(8,128)S(1)}, u32[]{:S(2)}) copy-start(f32[256,4,2304]{2,0,1:T(8,128)S(1)} %get-tuple-element.25) | copy-start | bytes 28311556
  64.6 9.6 %copy-start.2 = (f32[256,4,2304]{2,0,1:T(8,128)S(1)}, f32[256,4,2304]{2,0,1:T(8,128)}, u32[]{:S(2)}) copy-start(f32[256,4,2304]{2,0,1:T(8,128)} %copy-done.1) | copy-start | bytes 28311556
  77.1 3.7 %copy-start.5 = (bf16[256,4,2304]{2,0,1:T(8,128)(2,1)}, bf16[256,4,2304]{2,0,1:T(8,128)(2,1)S(1)}, u32[]{:S(2)}) copy-start(bf16[256,4,2304]{2,0,1:T(8,128)(2,1)S(1)} %fusion) | copy-start | bytes 14155780
  80.1 16.9 %copy-start.4 = (bf16[256,128]{0,1:T(8,128)(2,1)S(1)}, bf16[256,128]{0,1:T(8,128)(2,1)}, u32[]{:S(2)}) copy-start(bf16[256,128]{0,1:T(8,128)(2,1)} %fusion.26) | copy-start | bytes 196612
  80.4 18.0 %copy-start.3 = (bf16[256,128]{0,1:T(8,128)(2,1)S(1)}, bf16[256,128]{0,1:T(8,128)(2,1)}, u32[]{:S(2)}) copy-start(bf16[256,128]{0,1:T(8,128)(2,1)} %fusion.25) | copy-start | bytes 196612
  82.5 28.4 %all-to-all-start.2 = ((f32[32,8,512]{2,1,0:T(8,128)}), f32[32,8,512]{2,1,0:T(8,128)S(1)}, u32[]{:S(2)}, u32[]{:S(2)}) async-start(f32[32,8,512]{2,1,0:T(8,128)} %all_to_all.27), calls=%async_computation.2 | async-start | bytes 1048576 | tf_op jit(solution)/shard_map/all_to_all | solution.py:107
  90.5 10.7 %collective-permute-start.8 = (bf16[256,256]{0,1:T(8,128)(2,1)S(1)}, bf16[256,256]{0,1:T(8,128)(2,1)S(1)}, u32[]{:S(2)}, u32[]{:S(2)}) collective-permute-start(bf16[256,256]{0,1:T(8,128)(2,1)S(1)} %pad_maximum_fusion), channel_id=1, source_target_pairs={{32,0},{36,4},{40,8},{44,12},{48,16},{52,20},{56,24},{60,28},{64,3... | collective-permute-start | bytes 393224 | tf_op jit(solution)/shard_map/ppermute | solution.py:100
  91.8 13.3 %collective-permute-start.9 = (bf16[256,256]{0,1:T(8,128)(2,1)S(1)}, bf16[256,256]{0,1:T(8,128)(2,1)S(1)}, u32[]{:S(2)}, u32[]{:S(2)}) collective-permute-start(bf16[256,256]{0,1:T(8,128)(2,1)S(1)} %pad_maximum_fusion.1), channel_id=1, source_target_pairs={{28,0},{32,4},{36,8},{40,12},{44,16},{48,20},{52,24},{56,28},{60,3... | collective-permute-start | bytes 393224 | tf_op jit(solution)/shard_map/ppermute | solution.py:100
  93.1 15.9 %collective-permute-start.10 = (bf16[256,256]{0,1:T(8,128)(2,1)S(1)}, bf16[256,256]{0,1:T(8,128)(2,1)S(1)}, u32[]{:S(2)}, u32[]{:S(2)}) collective-permute-start(bf16[256,256]{0,1:T(8,128)(2,1)S(1)} %pad_maximum_fusion.2), channel_id=1, source_target_pairs={{24,0},{28,4},{32,8},{36,12},{40,16},{44,20},{48,24},{52,28},{56,3... | collective-permute-start | bytes 393224 | tf_op jit(solution)/shard_map/ppermute | solution.py:100
  94.5 31.0 %collective-permute-start.11 = (bf16[256,256]{0,1:T(8,128)(2,1)S(1)}, bf16[256,256]{0,1:T(8,128)(2,1)}, u32[]{:S(2)}, u32[]{:S(2)}) collective-permute-start(bf16[256,256]{0,1:T(8,128)(2,1)S(1)} %pad_maximum_fusion.3), channel_id=1, source_target_pairs={{20,0},{24,4},{28,8},{32,12},{36,16},{40,20},{44,24},{48,28},{52,3... | collective-permute-start | bytes 393224 | tf_op jit(solution)/shard_map/ppermute | solution.py:100
  95.8 29.7 %collective-permute-start.12 = (bf16[256,256]{0,1:T(8,128)(2,1)S(1)}, bf16[256,256]{0,1:T(8,128)(2,1)}, u32[]{:S(2)}, u32[]{:S(2)}) collective-permute-start(bf16[256,256]{0,1:T(8,128)(2,1)S(1)} %pad_maximum_fusion.4), channel_id=1, source_target_pairs={{16,0},{20,4},{24,8},{28,12},{32,16},{36,20},{40,24},{44,28},{48,3... | collective-permute-start | bytes 393224 | tf_op jit(solution)/shard_map/ppermute | solution.py:100
  101.2 24.3 %collective-permute-start.13 = (bf16[256,256]{0,1:T(8,128)(2,1)S(1)}, bf16[256,256]{0,1:T(8,128)(2,1)S(1)}, u32[]{:S(2)}, u32[]{:S(2)}) collective-permute-start(bf16[256,256]{0,1:T(8,128)(2,1)S(1)} %pad_maximum_fusion.5), channel_id=1, source_target_pairs={{12,0},{16,4},{20,8},{24,12},{28,16},{32,20},{36,24},{40,28},{44,3... | collective-permute-start | bytes 393224 | tf_op jit(solution)/shard_map/ppermute | solution.py:100
  105.1 20.4 %collective-permute-start.14 = (bf16[256,256]{0,1:T(8,128)(2,1)}, bf16[256,256]{0,1:T(8,128)(2,1)S(1)}, u32[]{:S(2)}, u32[]{:S(2)}) collective-permute-start(bf16[256,256]{0,1:T(8,128)(2,1)} %pad_maximum_fusion.6), channel_id=1, source_target_pairs={{8,0},{12,4},{16,8},{20,12},{24,16},{28,20},{32,24},{36,28},{40,32... | collective-permute-start | bytes 393224 | tf_op jit(solution)/shard_map/ppermute | solution.py:100
  109.0 16.5 %collective-permute-start.15 = (bf16[256,256]{0,1:T(8,128)(2,1)S(1)}, bf16[256,256]{0,1:T(8,128)(2,1)S(1)}, u32[]{:S(2)}, u32[]{:S(2)}) collective-permute-start(bf16[256,256]{0,1:T(8,128)(2,1)S(1)} %pad_maximum_fusion.7), channel_id=1, source_target_pairs={{4,0},{8,4},{12,8},{16,12},{20,16},{24,20},{28,24},{32,28},{36,32}... | collective-permute-start | bytes 393224 | tf_op jit(solution)/shard_map/ppermute | solution.py:100
  110.9 24.8 %all-to-all-start = ((f32[32,8,512]{2,1,0:T(8,128)}), f32[32,8,512]{2,1,0:T(8,128)S(1)}, u32[]{:S(2)}, u32[]{:S(2)}) async-start(f32[32,8,512]{2,1,0:T(8,128)} %all_to_all.22), calls=%async_computation | async-start | bytes 1048576 | tf_op jit(solution)/shard_map/all_to_all | solution.py:76
